TPU v7x, 128 devices: a whole 4x4x4 slice. The times are simulated.
128 devices in a mesh: row: 4 (over y), vocab: 32 (over z, x, core).
Axes of the slice: x: 4, y: 4, z: 4, core: 2. Of those that a mesh axis runs over, the one named last changes fastest.
Arguments:
- tokens: bfloat16 [1280, 7168], P(('row', 'vocab')), may hold values from -60 to 60
- norm_gain: float32 [7168], replicated, may hold values from 0.5 to 1.5
- router: bfloat16 [7168, 32], replicated, may hold values from -0.0625 to 0.0625
- routes: int32 [1280, 8], P(('row', 'vocab')), may hold values from 0 to 31, all different within a row; in each aligned block of 10 rows (0 to 9, 10 to 19, ...) at most 3 rows name the same one
- w_gate: bfloat16 [32, 7168, 1024], P('vocab', None, 'row'), may hold values from -0.0625 to 0.0625
- w_up: bfloat16 [32, 7168, 1024], P('vocab', None, 'row'), may hold values from -0.0625 to 0.0625
- w_down: bfloat16 [32, 1024, 7168], P('vocab', 'row'), may hold values from -0.1875 to 0.1875
- head_gain: float32 [7168], replicated, may hold values from 0.5 to 1.5
- head: bfloat16 [65536, 7168], P(('row', 'vocab')), may hold values from -0.18 to 0.18
- draft_logits: bfloat16 [256, 4, 65536], P(None, None, ('row', 'vocab')), may hold values from -18 to 235
- draft_tokens: int32 [256, 4], replicated, may hold values from 0 to 65535
- reject_pos: int32 [256], replicated, may hold values from 0 to 4
Outputs:
- residual: float32 [256, 65536], P(None, ('row', 'vocab'))
- accept: float32 [256, 4], replicated
Inputs may be any that keep to these rules, and one draw needn't show every extreme that they name: `routes`: each row names 8 different experts. Among the rows of one device no expert is named more than 3 times, and some device's rows name some expert exactly 3 times.
All inputs are finite; a program needn't handle non-finite values.
Results may differ from a plain program's by a relative error of at most 0.012.
Values may be sent and summed in bfloat16 or wider, within the bound.
No kernel may reach another device: no remote copies, remote signals or barrier semaphores. Data moves between devices by JAX's collectives and lax.ppermute only.
A program may use at most 256 MiB of HBM per device.

v0:
```python
import jax
import jax.numpy as jnp
import numpy as np
from jax import lax
from jax.sharding import Mesh
from jax.sharding import PartitionSpec as P

V = 65536
DRAFTS = 4
VOCAB_AXES = ("vz", "vx", "core")
ALL_AXES = ("row",) + VOCAB_AXES
RING_ORDER = ("core", "vx", "vz", "row")


def rms_norm(values, gain):
    return values * lax.rsqrt(jnp.mean(values * values, axis=-1, keepdims=True) + 1e-06) * gain


def tree_psum(values):
    for axis in RING_ORDER:
        values = lax.psum(values, axis)
    return values


def tree_pmax(values):
    for axis in RING_ORDER:
        values = lax.pmax(values, axis)
    return values


def body(
    tokens,
    norm_gain,
    router,
    routes,
    w_gate,
    w_up,
    w_down,
    head_gain,
    head,
    draft_logits,
    draft_tokens,
    reject_pos,
):
    vocab_count = 1
    for axis in VOCAB_AXES:
        vocab_count *= lax.axis_size(axis)
    row_count = lax.axis_size("row")
    rows_dev = tokens.shape[0]
    model_width = tokens.shape[1]
    top_k = routes.shape[1]
    experts = w_gate.shape[0] * vocab_count
    capacity = min(rows_dev, (rows_dev * top_k + experts - 1) // experts)
    local_vocab = head.shape[0]
    requests = draft_tokens.shape[0]
    slot_total = DRAFTS + 1
    offset = lax.axis_index(ALL_AXES) * local_vocab
    local_ids = draft_tokens - offset
    id_match = jnp.arange(local_vocab, dtype=jnp.int32)[None, None, :] == local_ids[:, :, None]
    draft_vals = draft_logits.astype(jnp.float32)
    top_draft = tree_pmax(jnp.max(draft_vals, axis=-1))
    draft_exp = jnp.exp(draft_vals - top_draft[:, :, None])
    sum_draft, pick_d = tree_psum(
        (jnp.sum(draft_exp, axis=-1), jnp.sum(jnp.where(id_match, draft_vals, 0.0), axis=-1))
    )
    resid_in = tokens.astype(jnp.float32)
    normed = rms_norm(resid_in, norm_gain).astype(jnp.bfloat16)
    scores = jax.nn.sigmoid(jnp.dot(normed, router, preferred_element_type=jnp.float32))
    member = routes[:, :, None] == jnp.arange(experts, dtype=jnp.int32)[None, None, :]
    chosen = jnp.any(member, axis=1)
    chosen_int = chosen.astype(jnp.int32)
    picked = chosen.astype(jnp.float32) * scores
    weights = 2.5 * picked / jnp.sum(picked, axis=1, keepdims=True)
    earlier = jnp.cumsum(chosen_int, axis=0) - chosen_int
    slot_ids = jnp.arange(capacity, dtype=jnp.int32)[None, :, None]
    selector = ((earlier.T[:, None, :] == slot_ids) & chosen.T[:, None, :]).astype(jnp.float32)
    send_buffer = jnp.einsum(
        "esr,rd->sed", selector.astype(jnp.bfloat16), normed, preferred_element_type=jnp.float32
    ).astype(jnp.bfloat16)
    gate_w = w_gate[0]
    up_w = w_up[0]
    down_w = w_down[0]
    received = lax.all_to_all(send_buffer, VOCAB_AXES, split_axis=1, concat_axis=1, tiled=True)
    shard_piece = lax.all_gather(received, "row", axis=1, tiled=True)
    flat_rows = shard_piece.reshape(-1, model_width)
    gate_out = jnp.dot(flat_rows, gate_w, preferred_element_type=jnp.float32)
    up_out = jnp.dot(flat_rows, up_w, preferred_element_type=jnp.float32)
    hidden = (jax.nn.silu(gate_out) * up_out).astype(jnp.bfloat16)
    down_out = jnp.dot(hidden, down_w, preferred_element_type=jnp.float32).astype(jnp.bfloat16)
    summed = lax.psum_scatter(
        down_out.reshape(shard_piece.shape), "row", scatter_dimension=1, tiled=True
    )
    returned = lax.all_to_all(summed, VOCAB_AXES, split_axis=1, concat_axis=1, tiled=True)
    combine = selector * weights.T[:, None, :]
    moe_sum = jnp.einsum(
        "esr,sed->rd", combine, returned.astype(jnp.float32), precision=lax.Precision.HIGHEST
    )
    mixed_rows = resid_in + moe_sum
    final_normed = rms_norm(mixed_rows, head_gain).astype(jnp.bfloat16)
    gathered = lax.all_gather(final_normed, ALL_AXES, axis=0, tiled=False)
    logits = jnp.einsum("gtd,wd->gtw", gathered, head, preferred_element_type=jnp.float32)
    target_logits = logits.reshape(requests, slot_total, local_vocab)
    pick_target = jnp.sum(jnp.where(id_match, target_logits[:, :DRAFTS], 0.0), axis=-1)
    top_target = tree_pmax(jnp.max(target_logits, axis=-1))
    target_exp = jnp.exp(target_logits - top_target[:, :, None])
    sum_target, pick_t = tree_psum((jnp.sum(target_exp, axis=-1), pick_target))
    target = target_exp / sum_target[:, :, None]
    draft_prob = draft_exp / sum_draft[:, :, None]
    log_target = pick_t - top_target[:, :DRAFTS] - jnp.log(sum_target[:, :DRAFTS])
    log_draft = pick_d - top_draft - jnp.log(sum_draft)
    accept = jnp.exp(jnp.minimum(log_target - log_draft, 0.0))
    position = (jnp.arange(slot_total, dtype=jnp.int32)[None, :] == reject_pos[:, None]).astype(
        jnp.float32
    )
    target_at = jnp.sum(position[:, :, None] * target, axis=1)
    draft_at = jnp.sum(position[:, :DRAFTS, None] * draft_prob, axis=1)
    gap_rows = jnp.maximum(target_at - draft_at, 0.0)
    gap_total = tree_psum(jnp.sum(gap_rows, axis=-1))
    residual = jnp.sqrt(V * gap_rows / gap_total[:, None])
    return (residual, accept)


def solution(mesh):
    row_size, vocab_size = mesh.devices.shape
    split = (row_size, 4, vocab_size // 8, 2)
    fine = Mesh(np.asarray(mesh.devices).reshape(split), ALL_AXES)
    spread = ALL_AXES
    placed = (
        P(spread, None),
        P(),
        P(),
        P(spread, None),
        P(VOCAB_AXES, None, "row"),
        P(VOCAB_AXES, None, "row"),
        P(VOCAB_AXES, "row", None),
        P(),
        P(spread, None),
        P(None, None, spread),
        P(),
        P(),
    )
    return jax.shard_map(
        body, mesh=fine, in_specs=placed, out_specs=(P(None, spread), P()), check_vma=False
    )
```

profile of v0, /device:TPU:0, one launch (start us, length us, event | category | flops | bytes accessed | tf_op | source)
XLA Modules:
  0.0 651.1 jit_solution(5099887849405684737)
XLA Ops:
  7.2 0.8 copy.62
  8.2 1.1 fusion.27
  9.3 1.5 fusion.2
  10.8 1.2 copy.63
  12.0 33.8 %all_to_all.10 = bf16[3,32,7168]{2,0,1:T(4,128)(2,1)S(1)} all-to-all(bf16[3,32,7168]{2,0,1:T(4,128)(2,1)S(1)} %copy.63), channel_id=1, replica_groups=mesh['row'=4,'vz'=4,'vx'=4,'core'=2] {'vz','vx','core'}, dimensions={1} | all-to-all | bytes 2752512 | tf_op jit(solution)/shard_map/all_to_all | solution.py:83
  45.9 1.7 copy.64
  47.5 0.5 all-reduce.15.cloned.1.call-start
  48.0 56.5 %all-gather.5.cloned.1.call-done = bf16[3,128,7168]{2,1,0:T(8,128)(2,1)} async-done(((bf16[3,32,7168]{2,1,0:T(8,128)(2,1)}), bf16[3,128,7168]{2,1,0:T(8,128)(2,1)}) %all-gather.5.cloned.1.call-update) | async-done | bytes 5505040 | tf_op jit(solution)/shard_map/all_gather | solution.py:84
  104.6 5.4 fusion.8
  110.0 0.9 copy-done.12
  110.9 1.6 fusion.21
  112.5 0.4 copy-done.5
  113.0 4.0 convolution_convert_fusion
  117.0 10.3 %copy.65 = bf16[3,128,7168]{2,0,1:T(4,128)(2,1)} copy(bf16[3,128,7168]{2,1,0:T(8,128)(2,1)} %bitcast.48) | data formatting | bytes 11010048 | tf_op jit(solution)/shard_map/reshape | solution.py:91
  127.3 0.6 copy-done.13
  127.9 0.6 dynamic-slice
  129.2 142.7 %all-reduce.15.cloned.1.call-done = bf16[3,128,7168]{2,0,1:T(4,128)(2,1)} async-done(((bf16[3,128,7168]{2,0,1:T(4,128)(2,1)}), bf16[3,128,7168]{2,0,1:T(4,128)(2,1)}) %all-reduce.15.cloned.1.call-update) | async-done | bytes 5505040
  271.9 3.5 constant_dynamic-slice_fusion
  275.3 7.4 %all-to-all-start.1 = ((bf16[3,32,7168]{2,0,1:T(4,128)(2,1)}), bf16[3,32,7168]{2,0,1:T(4,128)(2,1)S(1)}, u32[]{:S(2)}, u32[]{:S(2)}) async-start(bf16[3,32,7168]{2,0,1:T(4,128)(2,1)} %constant_dynamic-slice_fusion), calls=%async_computation.1 | async-start | bytes 3670016 | tf_op jit(solution)/shard_map/all_to_all | solution.py:93
  282.8 1.4 select_reduce_fusion
  284.2 25.5 %all-to-all-done.1 = bf16[3,32,7168]{2,0,1:T(4,128)(2,1)S(1)} async-done(((bf16[3,32,7168]{2,0,1:T(4,128)(2,1)}), bf16[3,32,7168]{2,0,1:T(4,128)(2,1)S(1)}, u32[]{:S(2)}, u32[]{:S(2)}) %all-to-all-start.1) | async-done | bytes 1376288 | tf_op jit(solution)/shard_map/all_to_all | solution.py:93
  309.7 2.3 multiply_reduce_fusion.1
  312.1 0.8 fusion.30
  312.9 0.8 copy.72
  313.7 0.5 reduce_max.27
  314.4 94.2 %all-gather.7.cloned.1.call-done = bf16[128,10,7168]{2,1,0:T(8,128)(2,1)} async-done(((bf16[1,10,7168]{2,1,0:T(8,128)(2,1)}), bf16[128,10,7168]{2,1,0:T(8,128)(2,1)}) %all-gather.7.cloned.1.call-update) | async-done | bytes 18350096 | tf_op jit(solution)/shard_map/all_gather | solution.py:100
  408.6 32.2 %fusion.53 = (f32[128,10]{0,1:T(8,128)S(1)}, f32[128,10,512]{2,0,1:T(8,128)S(1)}) fusion(bf16[512,7168]{1,0:T(8,128)(2,1)} %param.20, bf16[128,10,7168]{2,1,0:T(8,128)(2,1)} %all-gather.7.cloned.1.call-done), kind=kOutput, calls=%fused_computation.75 | convolution fusion | flops 9395895296 | bytes 28316672 | tf_op jit(solution)/shard_map/gtd,wd->gtw/dot_general | solution.py:101
  441.0 4.2 all-reduce.12
  445.2 20.1 %all-reduce.7 = (f32[256,5]{1,0:T(8,128)S(1)}, f32[256,4]{1,0:T(8,128)S(1)}) all-reduce(f32[256,5]{1,0:T(8,128)S(1)} %get-tuple-element.41, f32[256,4]{1,0:T(8,128)S(1)} %get-tuple-element.42), channel_id=1, replica_groups=mesh['row'=4,'vz'=4,'vx'=4,'core'=2] {'vx'}, use_global_device_ids=true, to_apply=%region_8.9 | all-reduce | flops 2304 | bytes 18432 | tf_op jit(solution)/shard_map/pmax | solution.py:27
  465.4 18.6 %all-reduce.8 = (f32[256,5]{1,0:T(8,128)S(1)}, f32[256,4]{1,0:T(8,128)S(1)}) all-reduce(f32[256,5]{1,0:T(8,128)S(1)} %get-tuple-element.30, f32[256,4]{1,0:T(8,128)S(1)} %get-tuple-element.31), channel_id=1, replica_groups=mesh['row'=4,'vz'=4,'vx'=4,'core'=2] {'vz'}, use_global_device_ids=true, to_apply=%region_9.10 | all-reduce | flops 2304 | bytes 18432 | tf_op jit(solution)/shard_map/pmax | solution.py:27
  484.0 19.0 %all-reduce.9 = (f32[256,5]{1,0:T(8,128)S(1)}, f32[256,4]{1,0:T(8,128)S(1)}) all-reduce(f32[256,5]{1,0:T(8,128)S(1)} %get-tuple-element.32, f32[256,4]{1,0:T(8,128)S(1)} %get-tuple-element.33), channel_id=1, replica_groups=mesh['row'=4,'vz'=4,'vx'=4,'core'=2] {'row'}, use_global_device_ids=true, to_apply=%region_10.11 | all-reduce | flops 2304 | bytes 18432 | tf_op jit(solution)/shard_map/pmax | solution.py:27
  503.2 3.6 copy.68
  506.8 0.7 exponential_reduce_fusion
  507.7 2.3 fusion.12
  510.0 4.8 reshape.70
  514.8 4.1 all-reduce.11
  518.9 18.1 %all-reduce.2 = (f32[256,5]{1,0:T(8,128)S(1)}, f32[256,4]{1,0:T(8,128)S(1)}) all-reduce(f32[256,5]{1,0:T(8,128)S(1)} %get-tuple-element.39, f32[256,4]{1,0:T(8,128)S(1)} %get-tuple-element.40), channel_id=1, replica_groups=mesh['row'=4,'vz'=4,'vx'=4,'core'=2] {'vx'}, use_global_device_ids=true, to_apply=%region_13.14 | all-reduce | flops 2304 | bytes 18432 | tf_op jit(solution)/shard_map/psum | solution.py:21
  537.0 17.8 %all-reduce.4 = (f32[256,5]{1,0:T(8,128)S(1)}, f32[256,4]{1,0:T(8,128)S(1)}) all-reduce(f32[256,5]{1,0:T(8,128)S(1)} %get-tuple-element.18, f32[256,4]{1,0:T(8,128)S(1)} %get-tuple-element.19), channel_id=1, replica_groups=mesh['row'=4,'vz'=4,'vx'=4,'core'=2] {'vz'}, use_global_device_ids=true, to_apply=%region_14.15 | all-reduce | flops 2304 | bytes 18432 | tf_op jit(solution)/shard_map/psum | solution.py:21
  554.8 17.0 %all-reduce.6 = (f32[256,5]{1,0:T(8,128)S(1)}, f32[256,4]{1,0:T(8,128)S(1)}) all-reduce(f32[256,5]{1,0:T(8,128)S(1)} %get-tuple-element.23, f32[256,4]{1,0:T(8,128)S(1)} %get-tuple-element.24), channel_id=1, replica_groups=mesh['row'=4,'vz'=4,'vx'=4,'core'=2] {'row'}, use_global_device_ids=true, to_apply=%region_15.16 | all-reduce | flops 2304 | bytes 18432 | tf_op jit(solution)/shard_map/psum | solution.py:21
  571.9 3.8 multiply_reduce_fusion
  575.8 5.6 fusion.14
  581.4 0.1 fusion.32
  581.5 4.7 all-reduce.10
  586.2 20.3 %all-reduce.1 = (f32[256]{0:T(256)S(1)}, f32[256,4]{1,0:T(8,128)S(1)}, f32[256,4]{1,0:T(8,128)S(1)}) all-reduce(f32[256]{0:T(256)S(1)} %get-tuple-element.36, f32[256,4]{1,0:T(8,128)S(1)} %get-tuple-element.37, f32[256,4]{1,0:T(8,128)S(1)} %get-tuple-element.38), channel_id=1, replica_groups=mesh['row'=4,'vz'=4,'vx'=4,'core'=2] {'vx'}, use_global_device_ids=true, to_apply=%region_30.31 | all-reduce | flops 2304 | bytes 18432 | tf_op jit(solution)/shard_map/psum | solution.py:21
  606.5 17.1 %all-reduce.3 = (f32[256]{0:T(256)S(1)}, f32[256,4]{1,0:T(8,128)S(1)}, f32[256,4]{1,0:T(8,128)S(1)}) all-reduce(f32[256]{0:T(256)S(1)} %get-tuple-element.15, f32[256,4]{1,0:T(8,128)S(1)} %get-tuple-element.16, f32[256,4]{1,0:T(8,128)S(1)} %get-tuple-element.17), channel_id=1, replica_groups=mesh['row'=4,'vz'=4,'vx'=4,'core'=2] {'vz'}, use_global_device_ids=true, to_apply=%region_31.32 | all-reduce | flops 2304 | bytes 18432 | tf_op jit(solution)/shard_map/psum | solution.py:21
  623.6 18.9 %all-reduce.5 = (f32[256]{0:T(256)S(1)}, f32[256,4]{1,0:T(8,128)S(1)}, f32[256,4]{1,0:T(8,128)S(1)}) all-reduce(f32[256]{0:T(256)S(1)} %get-tuple-element.20, f32[256,4]{1,0:T(8,128)S(1)} %get-tuple-element.21, f32[256,4]{1,0:T(8,128)S(1)} %get-tuple-element.22), channel_id=1, replica_groups=mesh['row'=4,'vz'=4,'vx'=4,'core'=2] {'row'}, use_global_device_ids=true, to_apply=%region_32.33 | all-reduce | flops 2304 | bytes 18432 | tf_op jit(solution)/shard_map/psum | solution.py:21
  642.6 0.7 copy.73
  643.3 1.0 divide_sqrt_fusion
  (46 shorter events, 1.1 us)
Async XLA Ops:
  7.2 275.6 %copy-start = (bf16[7168,32]{0,1:T(8,128)(2,1)S(1)}, bf16[7168,32]{0,1:T(8,128)(2,1)}, u32[]{:S(2)}) copy-start(bf16[7168,32]{0,1:T(8,128)(2,1)} %param.14) | copy-start | bytes 1376260
  7.2 97.4 %all-gather.5.cloned.1.call-start = ((), (), s32[]{:S(2)}) async-start(), calls=%async_computation.2 | async-start | bytes 6881280 | tf_op jit(solution)/shard_map/all_gather | solution.py:84
  47.5 224.3 %all-reduce.15.cloned.1.call-start = ((), (), s32[]{:S(2)}) async-start(), calls=%async_computation.4 | async-start | bytes 14680064
  104.6 5.4 copy-start.11
  104.6 6.3 copy-start.12
  110.9 2.0 copy-start.5
  127.3 0.7 copy-start.13
  129.2 153.6 %copy-start.7 = (f32[7168]{0:T(1024)S(1)}, f32[7168]{0:T(1024)}, u32[]{:S(2)}) copy-start(f32[7168]{0:T(1024)} %param.13) | copy-start | bytes 86020
  275.3 36.7 %copy-start.8 = (f32[7168]{0:T(1024)S(1)}, f32[7168]{0:T(1024)}, u32[]{:S(2)}) copy-start(f32[7168]{0:T(1024)} %param.19) | copy-start | bytes 86020
  275.3 37.6 %copy-start.9 = (s32[256,4]{0,1:T(4,128)S(1)}, s32[256,4]{0,1:T(4,128)}, u32[]{:S(2)}) copy-start(s32[256,4]{0,1:T(4,128)} %param.22) | copy-start | bytes 12292
  275.3 38.4 %copy-start.3 = (bf16[256,4,512]{2,1,0:T(4,128)(2,1)S(1)}, bf16[256,4,512]{2,1,0:T(4,128)(2,1)}, u32[]{:S(2)}) copy-start(bf16[256,4,512]{2,1,0:T(4,128)(2,1)} %param.21) | copy-start | bytes 3145732
  275.3 38.9 %copy-start.10 = (s32[256]{0:T(256)S(1)}, s32[256]{0:T(256)}, u32[]{:S(2)}) copy-start(s32[256]{0:T(256)} %param.23) | copy-start | bytes 3076
  275.3 34.4 %all-to-all-start.1 = ((bf16[3,32,7168]{2,0,1:T(4,128)(2,1)}), bf16[3,32,7168]{2,0,1:T(4,128)(2,1)S(1)}, u32[]{:S(2)}, u32[]{:S(2)}) async-start(bf16[3,32,7168]{2,0,1:T(4,128)(2,1)} %constant_dynamic-slice_fusion), calls=%async_computation.1 | async-start | bytes 3670016 | tf_op jit(solution)/shard_map/all_to_all | solution.py:93
  282.7 125.9 %all-gather.7.cloned.1.call-start = ((), (), s32[]{:S(2)}) async-start(), calls=%async_computation.3 | async-start | bytes 29589504 | tf_op jit(solution)/shard_map/all_gather | solution.py:100
  514.7 61.0 %copy-start.4 = (bf16[256,4,512]{2,1,0:T(4,128)(2,1)S(1)}, bf16[256,4,512]{2,1,0:T(4,128)(2,1)}, u32[]{:S(2)}) copy-start(bf16[256,4,512]{2,1,0:T(4,128)(2,1)} %param.21) | copy-start | bytes 3145732
  514.7 61.0 %copy-start.6 = (s32[256,4]{1,0:T(8,128)S(1)}, s32[256,4]{1,0:T(8,128)}, u32[]{:S(2)}) copy-start(s32[256,4]{1,0:T(8,128)} %copy.72) | copy-start | bytes 12292
  571.8 3.9 copy-start.2
  575.7 68.6 %copy-start.1 = (bf16[7168,32]{0,1:T(8,128)(2,1)S(1)}, bf16[7168,32]{0,1:T(8,128)(2,1)}, u32[]{:S(2)}) copy-start(bf16[7168,32]{0,1:T(8,128)(2,1)} %param.14) | copy-start | bytes 1376260
Sparse Core Ops, SparseCore 0:
  47.7 56.8 all-gather.4
  127.4 144.4 all-reduce.14
  313.0 95.5 all-gather.6
where the time goes:
time: 655 us; the launch traced here: 651 us
  waiting for transfers between devices  319 us (49%)
  blocking collectives  214 us (33%)
  matrix products  48.4 us (7%)
  local copies, waits for them, and re-layouts  30.4 us (5%)
  other arithmetic  16.4 us (3%)
  between operations  15 us (2%)
  starting transfers between devices  7.96 us (1%)
    unnamed x4, waiting for transfers between devices  143 us
    psum x8, blocking collectives, tree_psum(): values = lax.psum(values, axis)  118 us
    all_gather x1, waiting for transfers between devices, body(): gathered = lax.all_gather(final_normed, ALL_AXES, axis=0, tiled=False)  94.2 us
    pmax x4, blocking collectives, tree_pmax(): values = lax.pmax(values, axis)  62 us
    all_gather x1, waiting for transfers between devices, body(): shard_piece = lax.all_gather(received, 'row', axis=1, tiled=True)  56.5 us
    all_to_all x1, blocking collectives, body(): lax.all_to_all(send_buffer, VOCAB_AXES, split_axis=1, concat_axis=1, tile...  33.8 us
    dot_general x1, matrix products, body(): jnp.einsum('gtd,wd->gtw', gathered, head, preferred_element_type=jnp.floa...  32.2 us
    all_to_all x1, waiting for transfers between devices, body(): lax.all_to_all(summed, VOCAB_AXES, split_axis=1, concat_axis=1, tiled=True)  25.5 us
  transfers between devices with their start and end apart: 4, of which 4 were waited for; matrix products, arithmetic and copies ran while one was open for 1% of the time, Pallas kernels for 0%

commit v1 on v0

--- a/solution.py
+++ b/solution.py
@@ -4,12 +4,39 @@
 from jax import lax
 from jax.sharding import Mesh
 from jax.sharding import PartitionSpec as P
+from jax.lax import axis_index, axis_size, ppermute
 
 V = 65536
 DRAFTS = 4
 VOCAB_AXES = ("vz", "vx", "core")
 ALL_AXES = ("row",) + VOCAB_AXES
 RING_ORDER = ("core", "vx", "vz", "row")
+
+
+def mix_the_patches(payload, which_dim):
+    shard_axis = "row"
+    value_now = axis_size(shard_axis)
+    out_arr, z1, opened = (value_now, axis_index(shard_axis), payload.shape[which_dim])
+    inbox = [(q, (q + 1) % out_arr) for q in range(out_arr)]
+    tray = [(q, (q - 1) % out_arr) for q in range(out_arr)]
+    n_now = jnp.zeros(
+        (*payload.shape[:which_dim], out_arr * opened, *payload.shape[which_dim + 1 :]),
+        payload.dtype,
+    )
+    n_now = lax.dynamic_update_slice_in_dim(n_now, payload, z1 * opened, axis=which_dim)
+    view_out = res = payload
+    long_array = out_arr // 2
+    for dd in range(1, long_array + 1):
+        view_out = ppermute(view_out, axis_name=shard_axis, perm=inbox)
+        n_now = lax.dynamic_update_slice_in_dim(
+            n_now, view_out, (z1 - dd) % out_arr * opened, axis=which_dim
+        )
+        if dd < out_arr - long_array:
+            res = ppermute(res, axis_name=shard_axis, perm=tray)
+            n_now = lax.dynamic_update_slice_in_dim(
+                n_now, res, (z1 + dd) % out_arr * opened, axis=which_dim
+            )
+    return n_now
 
 
 def rms_norm(values, gain):
@@ -81,7 +108,7 @@
     up_w = w_up[0]
     down_w = w_down[0]
     received = lax.all_to_all(send_buffer, VOCAB_AXES, split_axis=1, concat_axis=1, tiled=True)
-    shard_piece = lax.all_gather(received, "row", axis=1, tiled=True)
+    shard_piece = mix_the_patches(received, 1)
     flat_rows = shard_piece.reshape(-1, model_width)
     gate_out = jnp.dot(flat_rows, gate_w, preferred_element_type=jnp.float32)
     up_out = jnp.dot(flat_rows, up_w, preferred_element_type=jnp.float32)

time: 655 us -> 667 us (1.018)
  blocking collectives: 214 us -> 180 us
  waiting for transfers between devices: 319 us -> 345 us
  starting transfers between devices: 7.96 us -> 19.7 us
  local copies, waits for them, and re-layouts: 30.4 us -> 38.3 us
    ppermute x0 -> x3, waiting for transfers between devices: none -> 58.3 us  [the longest x2 58.3 us: mix_the_patches(): view_out = ppermute(view_out, axis_name=shard_axis, perm=inbox)]
    all_gather x1 -> x0, waiting for transfers between devices: 56.5 us -> none  [body(): shard_piece = lax.all_gather(received, 'row', axis=1, tiled=True)]
    all_to_all x1 -> x0, blocking collectives: 33.8 us -> none  [body(): lax.all_to_all(send_buffer, VOCAB_AXES, split_axis=1, concat_axis=1, tile...]
    all_to_all x0 -> x1, waiting for transfers between devices: none -> 27 us  [body(): lax.all_to_all(send_buffer, VOCAB_AXES, split_axis=1, concat_axis=1, tile...]
    all_to_all x0 -> x1, starting transfers between devices: none -> 8.28 us  [body(): lax.all_to_all(send_buffer, VOCAB_AXES, split_axis=1, concat_axis=1, tile...]
    unnamed x4 -> x3, waiting for transfers between devices: 143 us -> 140 us
  transfers between devices with their start and end apart: 4 -> 7, of which waited for: 4 -> 6; matrix products, arithmetic and copies ran while one was open for 1% -> 1% of each run, Pallas kernels for 0% -> 0%
where the time goes in v1:
time: 667 us; the launch traced here: 662 us
  waiting for transfers between devices  345 us (52%)
  blocking collectives  180 us (27%)
  matrix products  47.4 us (7%)
  local copies, waits for them, and re-layouts  38.3 us (6%)
  starting transfers between devices  19.7 us (3%)
  other arithmetic  16.5 us (2%)
  between operations  15.3 us (2%)
    unnamed x3, waiting for transfers between devices  140 us
    psum x8, blocking collectives, tree_psum(): values = lax.psum(values, axis)  118 us
    all_gather x1, waiting for transfers between devices, body(): gathered = lax.all_gather(final_normed, ALL_AXES, axis=0, tiled=False)  94.2 us
    pmax x4, blocking collectives, tree_pmax(): values = lax.pmax(values, axis)  62 us
    ppermute x2, waiting for transfers between devices, mix_the_patches(): view_out = ppermute(view_out, axis_name=shard_axis, perm=inbox)  58.3 us
    dot_general x1, matrix products, body(): jnp.einsum('gtd,wd->gtw', gathered, head, preferred_element_type=jnp.floa...  32.2 us
    all_to_all x1, waiting for transfers between devices, body(): lax.all_to_all(send_buffer, VOCAB_AXES, split_axis=1, concat_axis=1, tile...  27 us
    all_to_all x1, waiting for transfers between devices, body(): lax.all_to_all(summed, VOCAB_AXES, split_axis=1, concat_axis=1, tiled=True)  25.5 us
  transfers between devices with their start and end apart: 7, of which 6 were waited for; matrix products, arithmetic and copies ran while one was open for 1% of the time, Pallas kernels for 0%

profile of v1, /device:TPU:0, one launch (start us, length us, event | category | flops | bytes accessed | tf_op | source)
XLA Modules:
  0.0 662.2 jit_solution(7420648498835805055)
XLA Ops:
  7.2 0.8 copy.66
  8.1 1.1 fusion.21
  9.3 1.5 fusion.2
  10.8 2.4 copy.67
  13.2 8.3 %all-to-all-start = ((bf16[3,32,7168]{2,0,1:T(4,128)(2,1)}), bf16[3,32,7168]{2,0,1:T(4,128)(2,1)S(1)}, u32[]{:S(2)}, u32[]{:S(2)}) async-start(bf16[3,32,7168]{2,0,1:T(4,128)(2,1)} %copy.67), calls=%async_computation | async-start | bytes 3670016 | tf_op jit(solution)/shard_map/all_to_all | solution.py:110
  21.6 27.0 %all-to-all-done = bf16[3,32,7168]{2,0,1:T(4,128)(2,1)S(1)} async-done(((bf16[3,32,7168]{2,0,1:T(4,128)(2,1)}), bf16[3,32,7168]{2,0,1:T(4,128)(2,1)S(1)}, u32[]{:S(2)}, u32[]{:S(2)}) %all-to-all-start) | async-done | bytes 1376288 | tf_op jit(solution)/shard_map/all_to_all | solution.py:110
  49.2 1.7 constant_dynamic-update-slice_fusion.3
  50.9 2.4 copy-done.5
  53.3 1.6 collective-permute-start
  54.9 1.7 collective-permute-start.1
  56.5 29.4 %collective-permute-done = bf16[3,32,7168]{2,1,0:T(8,128)(2,1)S(1)} collective-permute-done((bf16[3,32,7168]{2,1,0:T(8,128)(2,1)}, bf16[3,32,7168]{2,1,0:T(8,128)(2,1)S(1)}, u32[]{:S(2)}, u32[]{:S(2)}) %collective-permute-start) | collective-permute-done | bytes 1376288 | tf_op jit(solution)/shard_map/ppermute | solution.py:30
  86.7 1.2 constant_dynamic-update-slice_fusion.2
  87.9 1.2 constant_dynamic-update-slice_fusion.1
  89.1 28.9 %collective-permute-done.2 = bf16[3,32,7168]{2,1,0:T(8,128)(2,1)S(1)} collective-permute-done((bf16[3,32,7168]{2,1,0:T(8,128)(2,1)S(1)}, bf16[3,32,7168]{2,1,0:T(8,128)(2,1)S(1)}, u32[]{:S(2)}, u32[]{:S(2)}) %collective-permute-start.2) | collective-permute-done | bytes 1376288 | tf_op jit(solution)/shard_map/ppermute | solution.py:30
  118.0 1.2 constant_dynamic-update-slice_fusion
  119.2 4.3 fusion.6
  123.5 0.9 copy-done.14
  124.5 1.6 fusion.8
  126.5 4.0 convolution_convert_fusion
  130.5 10.3 %copy.71 = bf16[3,128,7168]{2,0,1:T(4,128)(2,1)} copy(bf16[3,128,7168]{2,1,0:T(8,128)(2,1)} %bitcast.43) | data formatting | bytes 11010048 | tf_op jit(solution)/shard_map/reshape | solution.py:118
  142.7 139.9 %all-reduce.15.cloned.1.call-done = bf16[3,128,7168]{2,0,1:T(4,128)(2,1)} async-done(((bf16[3,128,7168]{2,0,1:T(4,128)(2,1)}), bf16[3,128,7168]{2,0,1:T(4,128)(2,1)}) %all-reduce.15.cloned.1.call-update) | async-done | bytes 5505040
  282.6 3.5 constant_dynamic-slice_fusion
  286.1 7.4 %all-to-all-start.1 = ((bf16[3,32,7168]{2,0,1:T(4,128)(2,1)}), bf16[3,32,7168]{2,0,1:T(4,128)(2,1)S(1)}, u32[]{:S(2)}, u32[]{:S(2)}) async-start(bf16[3,32,7168]{2,0,1:T(4,128)(2,1)} %constant_dynamic-slice_fusion), calls=%async_computation.1 | async-start | bytes 3670016 | tf_op jit(solution)/shard_map/all_to_all | solution.py:120
  293.6 1.4 select_reduce_fusion
  295.0 25.5 %all-to-all-done.1 = bf16[3,32,7168]{2,0,1:T(4,128)(2,1)S(1)} async-done(((bf16[3,32,7168]{2,0,1:T(4,128)(2,1)}), bf16[3,32,7168]{2,0,1:T(4,128)(2,1)S(1)}, u32[]{:S(2)}, u32[]{:S(2)}) %all-to-all-start.1) | async-done | bytes 1376288 | tf_op jit(solution)/shard_map/all_to_all | solution.py:120
  320.5 2.3 multiply_reduce_fusion.1
  322.8 0.8 fusion.24
  323.7 0.8 copy.78
  325.1 94.2 %all-gather.4.cloned.1.call-done = bf16[128,10,7168]{2,1,0:T(8,128)(2,1)} async-done(((bf16[1,10,7168]{2,1,0:T(8,128)(2,1)}), bf16[128,10,7168]{2,1,0:T(8,128)(2,1)}) %all-gather.4.cloned.1.call-update) | async-done | bytes 18350096 | tf_op jit(solution)/shard_map/all_gather | solution.py:127
  419.4 32.2 %fusion.49 = (f32[128,10]{0,1:T(8,128)S(1)}, f32[128,10,512]{2,0,1:T(8,128)S(1)}) fusion(bf16[512,7168]{1,0:T(8,128)(2,1)} %param.20, bf16[128,10,7168]{2,1,0:T(8,128)(2,1)} %all-gather.4.cloned.1.call-done), kind=kOutput, calls=%fused_computation.80 | convolution fusion | flops 9395895296 | bytes 28316672 | tf_op jit(solution)/shard_map/gtd,wd->gtw/dot_general | solution.py:128
  451.8 4.2 all-reduce.12
  456.0 20.1 %all-reduce.7 = (f32[256,5]{1,0:T(8,128)S(1)}, f32[256,4]{1,0:T(8,128)S(1)}) all-reduce(f32[256,5]{1,0:T(8,128)S(1)} %get-tuple-element.41, f32[256,4]{1,0:T(8,128)S(1)} %get-tuple-element.42), channel_id=1, replica_groups=mesh['row'=4,'vz'=4,'vx'=4,'core'=2] {'vx'}, use_global_device_ids=true, to_apply=%region_8.9 | all-reduce | flops 2304 | bytes 18432 | tf_op jit(solution)/shard_map/pmax | solution.py:54
  476.2 18.6 %all-reduce.8 = (f32[256,5]{1,0:T(8,128)S(1)}, f32[256,4]{1,0:T(8,128)S(1)}) all-reduce(f32[256,5]{1,0:T(8,128)S(1)} %get-tuple-element.30, f32[256,4]{1,0:T(8,128)S(1)} %get-tuple-element.31), channel_id=1, replica_groups=mesh['row'=4,'vz'=4,'vx'=4,'core'=2] {'vz'}, use_global_device_ids=true, to_apply=%region_9.10 | all-reduce | flops 2304 | bytes 18432 | tf_op jit(solution)/shard_map/pmax | solution.py:54
  494.8 19.0 %all-reduce.9 = (f32[256,5]{1,0:T(8,128)S(1)}, f32[256,4]{1,0:T(8,128)S(1)}) all-reduce(f32[256,5]{1,0:T(8,128)S(1)} %get-tuple-element.32, f32[256,4]{1,0:T(8,128)S(1)} %get-tuple-element.33), channel_id=1, replica_groups=mesh['row'=4,'vz'=4,'vx'=4,'core'=2] {'row'}, use_global_device_ids=true, to_apply=%region_10.11 | all-reduce | flops 2304 | bytes 18432 | tf_op jit(solution)/shard_map/pmax | solution.py:54
  514.0 3.6 copy.74
  518.5 2.3 fusion.12
  520.8 4.8 reshape.70
  525.5 4.1 all-reduce.11
  529.7 18.1 %all-reduce.2 = (f32[256,5]{1,0:T(8,128)S(1)}, f32[256,4]{1,0:T(8,128)S(1)}) all-reduce(f32[256,5]{1,0:T(8,128)S(1)} %get-tuple-element.39, f32[256,4]{1,0:T(8,128)S(1)} %get-tuple-element.40), channel_id=1, replica_groups=mesh['row'=4,'vz'=4,'vx'=4,'core'=2] {'vx'}, use_global_device_ids=true, to_apply=%region_13.14 | all-reduce | flops 2304 | bytes 18432 | tf_op jit(solution)/shard_map/psum | solution.py:48
  547.8 17.8 %all-reduce.4 = (f32[256,5]{1,0:T(8,128)S(1)}, f32[256,4]{1,0:T(8,128)S(1)}) all-reduce(f32[256,5]{1,0:T(8,128)S(1)} %get-tuple-element.18, f32[256,4]{1,0:T(8,128)S(1)} %get-tuple-element.19), channel_id=1, replica_groups=mesh['row'=4,'vz'=4,'vx'=4,'core'=2] {'vz'}, use_global_device_ids=true, to_apply=%region_14.15 | all-reduce | flops 2304 | bytes 18432 | tf_op jit(solution)/shard_map/psum | solution.py:48
  565.6 17.0 %all-reduce.6 = (f32[256,5]{1,0:T(8,128)S(1)}, f32[256,4]{1,0:T(8,128)S(1)}) all-reduce(f32[256,5]{1,0:T(8,128)S(1)} %get-tuple-element.23, f32[256,4]{1,0:T(8,128)S(1)} %get-tuple-element.24), channel_id=1, replica_groups=mesh['row'=4,'vz'=4,'vx'=4,'core'=2] {'row'}, use_global_device_ids=true, to_apply=%region_15.16 | all-reduce | flops 2304 | bytes 18432 | tf_op jit(solution)/shard_map/psum | solution.py:48
  582.6 3.8 multiply_reduce_fusion
  586.5 5.6 fusion.14
  592.3 4.7 all-reduce.10
  597.0 20.3 %all-reduce.1 = (f32[256]{0:T(256)S(1)}, f32[256,4]{1,0:T(8,128)S(1)}, f32[256,4]{1,0:T(8,128)S(1)}) all-reduce(f32[256]{0:T(256)S(1)} %get-tuple-element.36, f32[256,4]{1,0:T(8,128)S(1)} %get-tuple-element.37, f32[256,4]{1,0:T(8,128)S(1)} %get-tuple-element.38), channel_id=1, replica_groups=mesh['row'=4,'vz'=4,'vx'=4,'core'=2] {'vx'}, use_global_device_ids=true, to_apply=%region_30.31 | all-reduce | flops 2304 | bytes 18432 | tf_op jit(solution)/shard_map/psum | solution.py:48
  617.3 17.1 %all-reduce.3 = (f32[256]{0:T(256)S(1)}, f32[256,4]{1,0:T(8,128)S(1)}, f32[256,4]{1,0:T(8,128)S(1)}) all-reduce(f32[256]{0:T(256)S(1)} %get-tuple-element.15, f32[256,4]{1,0:T(8,128)S(1)} %get-tuple-element.16, f32[256,4]{1,0:T(8,128)S(1)} %get-tuple-element.17), channel_id=1, replica_groups=mesh['row'=4,'vz'=4,'vx'=4,'core'=2] {'vz'}, use_global_device_ids=true, to_apply=%region_31.32 | all-reduce | flops 2304 | bytes 18432 | tf_op jit(solution)/shard_map/psum | solution.py:48
  634.4 18.9 %all-reduce.5 = (f32[256]{0:T(256)S(1)}, f32[256,4]{1,0:T(8,128)S(1)}, f32[256,4]{1,0:T(8,128)S(1)}) all-reduce(f32[256]{0:T(256)S(1)} %get-tuple-element.20, f32[256,4]{1,0:T(8,128)S(1)} %get-tuple-element.21, f32[256,4]{1,0:T(8,128)S(1)} %get-tuple-element.22), channel_id=1, replica_groups=mesh['row'=4,'vz'=4,'vx'=4,'core'=2] {'row'}, use_global_device_ids=true, to_apply=%region_32.33 | all-reduce | flops 2304 | bytes 18432 | tf_op jit(solution)/shard_map/psum | solution.py:48
  654.1 1.0 divide_sqrt_fusion
  (58 shorter events, 6.2 us)
Async XLA Ops:
  7.2 286.4 %copy-start = (bf16[7168,32]{0,1:T(8,128)(2,1)S(1)}, bf16[7168,32]{0,1:T(8,128)(2,1)}, u32[]{:S(2)}) copy-start(bf16[7168,32]{0,1:T(8,128)(2,1)} %param.14) | copy-start | bytes 1376260
  13.2 35.3 %all-to-all-start = ((bf16[3,32,7168]{2,0,1:T(4,128)(2,1)}), bf16[3,32,7168]{2,0,1:T(4,128)(2,1)S(1)}, u32[]{:S(2)}, u32[]{:S(2)}) async-start(bf16[3,32,7168]{2,0,1:T(4,128)(2,1)} %copy.67), calls=%async_computation | async-start | bytes 3670016 | tf_op jit(solution)/shard_map/all_to_all | solution.py:110
  21.5 261.1 %all-reduce.15.cloned.1.call-start = ((), (), s32[]{:S(2)}) async-start(), calls=%async_computation.3 | async-start | bytes 14680064
  50.9 2.4 copy-start.5
  53.3 32.6 %collective-permute-start = (bf16[3,32,7168]{2,1,0:T(8,128)(2,1)}, bf16[3,32,7168]{2,1,0:T(8,128)(2,1)S(1)}, u32[]{:S(2)}, u32[]{:S(2)}) collective-permute-start(bf16[3,32,7168]{2,1,0:T(8,128)(2,1)} %get-tuple-element.44), channel_id=1, source_target_pairs={{0,32},{32,64},{64,96},{96,0},{1,33},{33,65},{65,97},{97,1},{2,34}... | collective-permute-start | bytes 4128776 | tf_op jit(solution)/shard_map/ppermute | solution.py:30
  54.9 33.0 %collective-permute-start.1 = (bf16[3,32,7168]{2,1,0:T(8,128)(2,1)}, bf16[3,32,7168]{2,1,0:T(8,128)(2,1)S(1)}, u32[]{:S(2)}, u32[]{:S(2)}) collective-permute-start(bf16[3,32,7168]{2,1,0:T(8,128)(2,1)} %get-tuple-element.44), channel_id=1, source_target_pairs={{0,96},{32,0},{64,32},{96,64},{1,97},{33,1},{65,33},{97,65},{2,98}... | collective-permute-start | bytes 4128776 | tf_op jit(solution)/shard_map/ppermute | solution.py:35
  86.0 32.0 %collective-permute-start.2 = (bf16[3,32,7168]{2,1,0:T(8,128)(2,1)S(1)}, bf16[3,32,7168]{2,1,0:T(8,128)(2,1)S(1)}, u32[]{:S(2)}, u32[]{:S(2)}) collective-permute-start(bf16[3,32,7168]{2,1,0:T(8,128)(2,1)S(1)} %collective-permute-done), channel_id=1, source_target_pairs={{0,32},{32,64},{64,96},{96,0},{1,33},{33,65},{65,97},{97,1},{2,34}... | collective-permute-start | bytes 4128776 | tf_op jit(solution)/shard_map/ppermute | solution.py:30
  86.7 32.5 %copy-start.13 = (bf16[1,7168,256]{2,1,0:T(8,128)(2,1)S(1)}, bf16[1,7168,256]{2,1,0:T(8,128)(2,1)}, u32[]{:S(2)}) copy-start(bf16[1,7168,256]{2,1,0:T(8,128)(2,1)} %param.17) | copy-start | bytes 11010052
  119.2 4.4 copy-start.6
  119.2 5.3 copy-start.14
  124.5 2.0 copy-start.7
  140.8 0.7 copy-start.15
  142.7 150.9 %copy-start.9 = (f32[7168]{0:T(1024)S(1)}, f32[7168]{0:T(1024)}, u32[]{:S(2)}) copy-start(f32[7168]{0:T(1024)} %param.13) | copy-start | bytes 86020
  286.1 36.7 %copy-start.10 = (f32[7168]{0:T(1024)S(1)}, f32[7168]{0:T(1024)}, u32[]{:S(2)}) copy-start(f32[7168]{0:T(1024)} %param.19) | copy-start | bytes 86020
  286.1 37.6 %copy-start.11 = (s32[256,4]{0,1:T(4,128)S(1)}, s32[256,4]{0,1:T(4,128)}, u32[]{:S(2)}) copy-start(s32[256,4]{0,1:T(4,128)} %param.22) | copy-start | bytes 12292
  286.1 38.4 %copy-start.3 = (bf16[256,4,512]{2,1,0:T(4,128)(2,1)S(1)}, bf16[256,4,512]{2,1,0:T(4,128)(2,1)}, u32[]{:S(2)}) copy-start(bf16[256,4,512]{2,1,0:T(4,128)(2,1)} %param.21) | copy-start | bytes 3145732
  286.1 38.9 %copy-start.12 = (s32[256]{0:T(256)S(1)}, s32[256]{0:T(256)}, u32[]{:S(2)}) copy-start(s32[256]{0:T(256)} %param.23) | copy-start | bytes 3076
  286.1 34.4 %all-to-all-start.1 = ((bf16[3,32,7168]{2,0,1:T(4,128)(2,1)}), bf16[3,32,7168]{2,0,1:T(4,128)(2,1)S(1)}, u32[]{:S(2)}, u32[]{:S(2)}) async-start(bf16[3,32,7168]{2,0,1:T(4,128)(2,1)} %constant_dynamic-slice_fusion), calls=%async_computation.1 | async-start | bytes 3670016 | tf_op jit(solution)/shard_map/all_to_all | solution.py:120
  293.5 125.9 %all-gather.4.cloned.1.call-start = ((), (), s32[]{:S(2)}) async-start(), calls=%async_computation.2 | async-start | bytes 29589504 | tf_op jit(solution)/shard_map/all_gather | solution.py:127
  525.5 61.0 %copy-start.4 = (bf16[256,4,512]{2,1,0:T(4,128)(2,1)S(1)}, bf16[256,4,512]{2,1,0:T(4,128)(2,1)}, u32[]{:S(2)}) copy-start(bf16[256,4,512]{2,1,0:T(4,128)(2,1)} %param.21) | copy-start | bytes 3145732
  525.5 61.0 %copy-start.8 = (s32[256,4]{1,0:T(8,128)S(1)}, s32[256,4]{1,0:T(8,128)}, u32[]{:S(2)}) copy-start(s32[256,4]{1,0:T(8,128)} %copy.78) | copy-start | bytes 12292
  582.6 3.9 copy-start.2
  586.5 68.6 %copy-start.1 = (bf16[7168,32]{0,1:T(8,128)(2,1)S(1)}, bf16[7168,32]{0,1:T(8,128)(2,1)}, u32[]{:S(2)}) copy-start(bf16[7168,32]{0,1:T(8,128)(2,1)} %param.14) | copy-start | bytes 1376260
Sparse Core Ops, SparseCore 0:
  141.0 141.6 all-reduce.14
  323.8 95.5 all-gather.3
